TPU v7x, 32 devices: a whole 2x2x4 slice. The times are simulated.
32 devices in a mesh: row: 8 (over y, x, core), col: 4 (over z).
Axes of the slice: x: 2, y: 2, z: 4, core: 2. Of those that a mesh axis runs over, the one named last changes fastest.
Arguments:
- tokens: bfloat16 [192, 8192], P('col', 'row'), may hold values from -6 to 6
- grad_out: bfloat16 [192, 8192], P('col', 'row'), may hold values from -6 to 6
- gate_weight: bfloat16 [8192, 14336], P('row', 'col'), may hold values from -0.0625 to 0.0625
- up_weight: bfloat16 [8192, 14336], P('row', 'col'), may hold values from -0.0625 to 0.0625
- down_weight: bfloat16 [14336, 8192], P('col', 'row'), may hold values from -0.046875 to 0.046875
Outputs:
- grad_tokens: bfloat16 [192, 8192], P('col', 'row')
- grad_gate_weight: bfloat16 [8192, 14336], P('row', 'col')
- grad_up_weight: bfloat16 [8192, 14336], P('row', 'col')
- grad_down_weight: bfloat16 [14336, 8192], P('col', 'row')
All inputs are finite; a program needn't handle non-finite values.
Results may differ from a plain program's by a relative error of at most 0.024.
Values may be sent and summed in bfloat16 or wider, within the bound.
No kernel may reach another device: no remote copies, remote signals or barrier semaphores. Data moves between devices by JAX's collectives and lax.ppermute only.
A program may use at most 128 MiB of HBM per device.

v0:
```python
import jax
import jax.numpy as jnp
from jax import lax
from jax.sharding import PartitionSpec as P


def contract_first(left, right):
    return lax.dot_general(
        left, right, (((0,), (0,)), ((), ())), preferred_element_type=jnp.float32
    )


def contract_last(left, right):
    return lax.dot_general(
        left, right, (((1,), (1,)), ((), ())), preferred_element_type=jnp.float32
    )


def gated_grads(gate_sum, up_sum, grad_hidden):
    sigmoid_gate = jax.nn.sigmoid(gate_sum)
    hidden = (gate_sum * sigmoid_gate * up_sum).astype(jnp.bfloat16)
    grad_up = (grad_hidden * gate_sum * sigmoid_gate).astype(jnp.bfloat16)
    grad_gate = (
        grad_hidden * up_sum * sigmoid_gate * (1.0 + gate_sum * (1.0 - sigmoid_gate))
    ).astype(jnp.bfloat16)
    return (hidden, grad_gate, grad_up)


def body(tokens, grad_out, gate_weight, up_weight, down_weight):
    tok_all, grad_all = (
        lax.all_gather(tokens, "col", axis=0, tiled=True),
        lax.all_gather(grad_out, "col", axis=0, tiled=True),
    )
    gate_sum, up_sum, grad_hidden = (
        lax.psum(
            jnp.dot(tok_all, gate_weight, preferred_element_type=jnp.float32).astype(jnp.bfloat16),
            "row",
        ).astype(jnp.float32),
        lax.psum(
            jnp.dot(tok_all, up_weight, preferred_element_type=jnp.float32).astype(jnp.bfloat16),
            "row",
        ).astype(jnp.float32),
        lax.psum(contract_last(grad_all, down_weight).astype(jnp.bfloat16), "row").astype(
            jnp.float32
        ),
    )
    hidden, grad_gate, grad_up = gated_grads(gate_sum, up_sum, grad_hidden)
    acc_gate = contract_first(tok_all, grad_gate)
    acc_up = contract_first(tok_all, grad_up)
    acc_down = contract_first(hidden, grad_all)
    partial_grad = contract_last(grad_gate, gate_weight) + contract_last(grad_up, up_weight)
    grad_tokens = lax.psum_scatter(
        partial_grad.astype(jnp.bfloat16), "col", scatter_dimension=0, tiled=True
    )
    return (
        grad_tokens,
        acc_gate.astype(jnp.bfloat16),
        acc_up.astype(jnp.bfloat16),
        acc_down.astype(jnp.bfloat16),
    )


def solution(mesh):
    return jax.shard_map(
        body,
        mesh=mesh,
        in_specs=(
            P("col", "row"),
            P("col", "row"),
            P("row", "col"),
            P("row", "col"),
            P("col", "row"),
        ),
        out_specs=(P("col", "row"), P("row", "col"), P("row", "col"), P("col", "row")),
        check_vma=False,
    )
```

profile of v0, /device:TPU:0, one launch (start us, length us, event | category | flops | bytes accessed | tf_op | source)
XLA Modules:
  0.0 188.0 jit_solution(11670191383653160460)
XLA Ops:
  7.2 0.0 all-reduce.3.cloned.1.call-start
  7.2 16.5 %all_gather.7 = bf16[192,1024]{1,0:T(8,128)(2,1)S(1)} all-gather(bf16[48,1024]{1,0:T(8,128)(2,1)} %param.5), channel_id=1, replica_groups=mesh['row'=8,'col'=4] {'col'}, dimensions={0}, use_global_device_ids=true | all-gather | bytes 491520 | tf_op jit(solution)/shard_map/all_gather | solution.py:31
  23.7 15.8 %all_gather.6 = bf16[192,1024]{1,0:T(8,128)(2,1)S(1)} all-gather(bf16[48,1024]{1,0:T(8,128)(2,1)} %param.6), channel_id=1, replica_groups=mesh['row'=8,'col'=4] {'col'}, dimensions={0}, use_global_device_ids=true | all-gather | bytes 491520 | tf_op jit(solution)/shard_map/all_gather | solution.py:32
  39.4 5.9 %convolution_convert_fusion.4 = bf16[192,3584]{1,0:T(8,128)(2,1)} fusion(bf16[192,1024]{1,0:T(8,128)(2,1)S(1)} %all_gather.7, bf16[1024,3584]{1,0:T(8,128)(2,1)} %param.8), kind=kOutput, calls=%fused_computation.6 | convolution fusion | flops 1409974272 | bytes 9109504 | tf_op jit(solution)/shard_map/dot_general | solution.py:40
  45.4 0.0 copy-done.4
  45.4 2.7 %convolution_convert_fusion.3 = bf16[192,3584]{1,0:T(8,128)(2,1)} fusion(bf16[192,1024]{1,0:T(8,128)(2,1)S(1)} %all_gather.7, bf16[1024,3584]{1,0:T(8,128)(2,1)S(1)} %copy-done.4), kind=kOutput, calls=%fused_computation.5 | convolution fusion | flops 1409974272 | bytes 9109504 | tf_op jit(solution)/shard_map/dot_general | solution.py:36
  48.1 0.0 slice-done
  48.1 0.0 slice-done.1
  48.1 3.6 %convolution_convert_fusion.5 = bf16[192,3584]{1,0:T(8,128)(2,1)} fusion(bf16[192,1024]{1,0:T(8,128)(2,1)S(1)} %all_gather.6, bf16[3584,1024]{1,0:T(8,128)(2,1)S(1)} %bitcast.18), kind=kOutput, calls=%fused_computation.7 | convolution fusion | flops 1409974272 | bytes 9109504 | tf_op jit(solution)/shard_map/dot_general | solution.py:14
  51.7 0.0 all-reduce.3.cloned.1.call-update
  51.7 0.2 reduce-scatter.2.cloned.1.call-start
  51.9 81.2 %all-reduce.3.cloned.1.call-done = (bf16[192,3584]{1,0:T(8,128)(2,1)}, bf16[192,3584]{1,0:T(8,128)(2,1)}, bf16[192,3584]{1,0:T(8,128)(2,1)}) async-done(((bf16[192,3584]{1,0:T(8,128)(2,1)}, bf16[192,3584]{1,0:T(8,128)(2,1)}, bf16[192,3584]{1,0:T(8,128)(2,1)}), (bf16[192,3584]{1,0:T(8,128)(2,1)}, bf16[192,3584]{1,0:T(8,128)(2,1)}, bf16[192,3584]{1,0:T(8,128)(2,1)})) %all-reduce.3.cloned.1.call-update) | async-done | bytes 4128784 | tf_op jit(solution)/shard_map/psum | solution.py:39
  133.2 7.0 %fusion.1 = bf16[1024,3584]{0,1:T(8,128)(2,1)} fusion(bf16[192,1024]{1,0:T(8,128)(2,1)S(1)} %all_gather.7, bf16[192,3584]{1,0:T(8,128)(2,1)} %get-tuple-element.10, bf16[192,3584]{1,0:T(8,128)(2,1)} %get-tuple-element.9), kind=kOutput, calls=%fused_computation.4 | convolution fusion | flops 1418461184 | bytes 10485760 | tf_op jit(solution)/shard_map/dot_general | solution.py:8
  140.2 0.0 copy-done
  140.2 0.0 slice-start.2
  140.3 1.2 fusion.4
  141.5 0.0 slice-start.3
  141.5 5.7 %fusion.18 = f32[192,1024]{1,0:T(8,128)S(1)} fusion(bf16[192,3584]{1,0:T(8,128)(2,1)S(1)} %fusion.4, bf16[1024,3584]{1,0:T(8,128)(2,1)} %param.7), kind=kOutput, calls=%fused_computation.28 | convolution fusion | flops 1409286144 | bytes 9502720 | tf_op jit(solution)/shard_map/dot_general | solution.py:14
  147.3 3.4 %fusion.14 = bf16[192,1024]{1,0:T(8,128)(2,1)} fusion(f32[192,1024]{1,0:T(8,128)S(1)} %fusion.18, bf16[1024,3584]{1,0:T(8,128)(2,1)S(1)} %bitcast.20, bf16[192,3584]{1,0:T(8,128)(2,1)S(1)} %copy-done.1, bf16[192,3584]{1,0:T(8,128)(2,1)S(1)} %copy-done.3), kind=kOutput, calls=%fused_computation.26 | convolution fusion | flops 1415184384 | bytes 11272192 | tf_op jit(solution)/shard_map/dot_general | solution.py:14
  150.6 0.0 reduce-scatter.2.cloned.1.call-update
  150.7 5.2 %fusion = bf16[1024,3584]{0,1:T(8,128)(2,1)} fusion(bf16[192,3584]{1,0:T(8,128)(2,1)S(1)} %fusion.4, bf16[192,1024]{1,0:T(8,128)(2,1)S(1)} %all_gather.7), kind=kOutput, calls=%fused_computation.3 | convolution fusion | flops 1412956160 | bytes 9109504 | tf_op jit(solution)/shard_map/dot_general | solution.py:8
  155.8 10.0 %copy.9 = bf16[1024,3584]{1,0:T(8,128)(2,1)} copy(bf16[1024,3584]{0,1:T(8,128)(2,1)} %fusion) | data formatting | bytes 14680064
  165.8 10.0 %copy.10 = bf16[1024,3584]{1,0:T(8,128)(2,1)} copy(bf16[1024,3584]{0,1:T(8,128)(2,1)} %fusion.1) | data formatting | bytes 14680064
  175.8 5.3 %convolution_convert_fusion = bf16[3584,1024]{1,0:T(8,128)(2,1)} fusion(bf16[192,1024]{1,0:T(8,128)(2,1)S(1)} %all_gather.6, bf16[192,3584]{1,0:T(8,128)(2,1)S(1)} %copy-done, bf16[192,3584]{1,0:T(8,128)(2,1)S(1)} %copy-done.2), kind=kOutput, calls=%fused_computation | convolution fusion | flops 1418461184 | bytes 10485760 | tf_op jit(solution)/shard_map/dot_general | solution.py:8
  (15 shorter events, 0.0 us)
Async XLA Ops:
  7.2 126.0 %all-reduce.3.cloned.1.call-start = ((), (), s32[]{:S(2)}) async-start(), calls=%async_computation.2 | async-start | bytes 8257536 | tf_op jit(solution)/shard_map/psum | solution.py:39
  39.4 5.9 %copy-start.4 = (bf16[1024,3584]{1,0:T(8,128)(2,1)S(1)}, bf16[1024,3584]{1,0:T(8,128)(2,1)}, u32[]{:S(2)}) copy-start(bf16[1024,3584]{1,0:T(8,128)(2,1)} %param.7) | copy-start | bytes 22020100
  39.4 8.6 %slice-start = ((s8[7340032]{0:T(1024)(128)(4,1)}), s8[4194304]{0:T(1024)(128)(4,1)S(1)}, s32[]{:S(2)}) async-start(s8[7340032]{0:T(1024)(128)(4,1)} %bitcast.17), calls=%async_computation.3 | async-start | bytes 8388608
  45.4 2.7 %slice-start.1 = ((s8[7340032]{0:T(1024)(128)(4,1)}), s8[3145728]{0:T(1024)(128)(4,1)S(1)}, s32[]{:S(2)}) async-start(s8[7340032]{0:T(1024)(128)(4,1)} %bitcast.17), calls=%async_computation.4 | async-start | bytes 6291456
  51.7 129.4 %reduce-scatter.2.cloned.1.call-start = ((), (), s32[]{:S(2)}) async-start(), calls=%async_computation.1 | async-start | bytes 491520 | tf_op jit(solution)/shard_map/reduce_scatter | solution.py:52
  133.2 7.1 %copy-start = (bf16[192,3584]{1,0:T(8,128)(2,1)S(1)}, bf16[192,3584]{1,0:T(8,128)(2,1)}, u32[]{:S(2)}) copy-start(bf16[192,3584]{1,0:T(8,128)(2,1)} %get-tuple-element.8) | copy-start | bytes 4128772
  133.2 7.1 %copy-start.1 = (bf16[192,3584]{1,0:T(8,128)(2,1)S(1)}, bf16[192,3584]{1,0:T(8,128)(2,1)}, u32[]{:S(2)}) copy-start(bf16[192,3584]{1,0:T(8,128)(2,1)} %get-tuple-element.10) | copy-start | bytes 4128772
  133.2 7.1 %copy-start.3 = (bf16[192,3584]{1,0:T(8,128)(2,1)S(1)}, bf16[192,3584]{1,0:T(8,128)(2,1)}, u32[]{:S(2)}) copy-start(bf16[192,3584]{1,0:T(8,128)(2,1)} %get-tuple-element.9) | copy-start | bytes 4128772
  140.2 7.0 %slice-start.2 = ((s8[7340032]{0:T(1024)(128)(4,1)}), s8[4194304]{0:T(1024)(128)(4,1)S(1)}, s32[]{:S(2)}) async-start(s8[7340032]{0:T(1024)(128)(4,1)} %bitcast.19), calls=%async_computation.5 | async-start | bytes 8388608
  141.5 5.8 %slice-start.3 = ((s8[7340032]{0:T(1024)(128)(4,1)}), s8[3145728]{0:T(1024)(128)(4,1)S(1)}, s32[]{:S(2)}) async-start(s8[7340032]{0:T(1024)(128)(4,1)} %bitcast.19), calls=%async_computation.6 | async-start | bytes 6291456
  165.8 10.0 %copy-start.2 = (bf16[192,3584]{1,0:T(8,128)(2,1)S(1)}, bf16[192,3584]{1,0:T(8,128)(2,1)}, u32[]{:S(2)}) copy-start(bf16[192,3584]{1,0:T(8,128)(2,1)} %get-tuple-element.10) | copy-start | bytes 4128772
Sparse Core Ops, SparseCore 0:
  51.8 81.3 all-reduce.2
  150.8 20.8 reduce-scatter.1
where the time goes:
time: 189 us; the launch traced here: 188 us
  waiting for transfers between devices  81.3 us (43%)
  matrix products  38.8 us (21%)
  blocking collectives  32.2 us (17%)
  local copies, waits for them, and re-layouts  20.1 us (11%)
  between operations  14.1 us (7%)
    psum x1, waiting for transfers between devices, body(): lax.psum(jnp.dot(tok_all, up_weight, preferred_element_type=jnp.float32)....  81.2 us
    unnamed x20, local copies, waits for them, and re-layouts  20.1 us
    dot_general x3, matrix products, contract_first(): lax.dot_general(left, right, (((0,), (0,)), ((), ())), preferred_element_...  17.5 us
    all_gather x1, blocking collectives, body(): lax.all_gather(tokens, 'col', axis=0, tiled=True)  16.5 us
    all_gather x1, blocking collectives, body(): lax.all_gather(grad_out, 'col', axis=0, tiled=True)  15.8 us
    dot_general x3, matrix products, contract_last(): lax.dot_general(left, right, (((1,), (1,)), ((), ())), preferred_element_...  12.7 us
    dot_general x1, matrix products, body(): jnp.dot(tok_all, up_weight, preferred_element_type=jnp.float32)  5.91 us
  transfers between devices with their start and end apart: 2, of which 1 were waited for; matrix products, arithmetic and copies ran while one was open for 16% of the time, Pallas kernels for 0%

commit v1 on v0

--- a/solution.py
+++ b/solution.py
@@ -2,6 +2,28 @@
 import jax.numpy as jnp
 from jax import lax
 from jax.sharding import PartitionSpec as P
+
+
+def in_order(tiles, dim):
+    tiles = jnp.moveaxis(tiles, 0, dim)
+    dims = tiles.shape
+    return tiles.reshape(*dims[:dim], dims[dim] * dims[dim + 1], *dims[dim + 2 :])
+
+
+def collected_by_bits(x, axis):
+    size = lax.axis_size(axis)
+    pieces = x[None]
+    for level in range(size.bit_length() - 1):
+        apart = 1 << level
+        other = lax.ppermute(pieces, axis, [(i, i ^ apart) for i in range(size)])
+        both = jnp.stack([pieces, other])
+        upper = lax.axis_index(axis) >> level & 1
+        pieces = jnp.where(upper == 0, both, both[::-1]).reshape(-1, *x.shape)
+    return pieces
+
+
+def doubled_up(shard, axis, dim):
+    return in_order(collected_by_bits(shard, axis), dim)
 
 
 def contract_first(left, right):
@@ -29,7 +51,7 @@
 def body(tokens, grad_out, gate_weight, up_weight, down_weight):
     tok_all, grad_all = (
         lax.all_gather(tokens, "col", axis=0, tiled=True),
-        lax.all_gather(grad_out, "col", axis=0, tiled=True),
+        doubled_up(grad_out, "col", 0),
     )
     gate_sum, up_sum, grad_hidden = (
         lax.psum(

time: 189 us -> 183 us (0.968)
  blocking collectives: 32.2 us -> 14.8 us
  matrix products: 38.8 us -> 44.9 us
  starting transfers between devices: 0.26 us -> 4.13 us
    all_gather x1 -> x0, blocking collectives: 15.8 us -> none  [body(): lax.all_gather(grad_out, 'col', axis=0, tiled=True)]
    ppermute x0 -> x2, starting transfers between devices: none -> 3.87 us  [collected_by_bits(): other = lax.ppermute(pieces, axis, [(i, i ^ apart) for i in range(size)])]
    dot_general x3, matrix products: 12.7 us -> 15.8 us  [contract_last(): lax.dot_general(left, right, (((1,), (1,)), ((), ())), preferred_element_...]
    dot_general x1, matrix products: 2.7 us -> 5.76 us  [body(): jnp.dot(tok_all, gate_weight, preferred_element_type=jnp.float32)]
    ppermute x0 -> x2, waiting for transfers between devices: none -> 2.23 us  [collected_by_bits(): other = lax.ppermute(pieces, axis, [(i, i ^ apart) for i in range(size)])]
    unnamed x20 -> x16, local copies, waits for them, and re-layouts: 20.1 us -> 20.1 us
  transfers between devices with their start and end apart: 2 -> 4, of which waited for: 1 -> 2; matrix products, arithmetic and copies ran while one was open for 16% -> 23% of each run, Pallas kernels for 0% -> 0%
where the time goes in v1:
time: 183 us; the launch traced here: 182 us
  waiting for transfers between devices  82.6 us (45%)
  matrix products  44.9 us (25%)
  local copies, waits for them, and re-layouts  20.1 us (11%)
  blocking collectives  14.8 us (8%)
  between operations  14.1 us (8%)
  starting transfers between devices  4.13 us (2%)
    psum x1, waiting for transfers between devices, body(): lax.psum(jnp.dot(tok_all, up_weight, preferred_element_type=jnp.float32)....  80.4 us
    unnamed x16, local copies, waits for them, and re-layouts  20.1 us
    dot_general x3, matrix products, contract_first(): lax.dot_general(left, right, (((0,), (0,)), ((), ())), preferred_element_...  17.5 us
    dot_general x3, matrix products, contract_last(): lax.dot_general(left, right, (((1,), (1,)), ((), ())), preferred_element_...  15.8 us
    all_gather x1, blocking collectives, body(): lax.all_gather(tokens, 'col', axis=0, tiled=True)  14.8 us
    dot_general x1, matrix products, body(): jnp.dot(tok_all, up_weight, preferred_element_type=jnp.float32)  5.8 us
    dot_general x1, matrix products, body(): jnp.dot(tok_all, gate_weight, preferred_element_type=jnp.float32)  5.76 us
    ppermute x2, starting transfers between devices, collected_by_bits(): other = lax.ppermute(pieces, axis, [(i, i ^ apart) for i in range(size)])  3.87 us
  transfers between devices with their start and end apart: 4, of which 2 were waited for; matrix products, arithmetic and copies ran while one was open for 23% of the time, Pallas kernels for 0%

profile of v1, /device:TPU:0, one launch (start us, length us, event | category | flops | bytes accessed | tf_op | source)
XLA Modules:
  0.0 182.0 jit_solution(12897079581404501808)
XLA Ops:
  7.2 0.0 all-reduce.3.cloned.1.call-start
  7.2 3.1 %collective-permute-start = (bf16[1,48,1024]{2,1,0:T(8,128)(2,1)}, bf16[1,48,1024]{2,1,0:T(8,128)(2,1)S(1)}, u32[]{:S(2)}, u32[]{:S(2)}) collective-permute-start(bf16[1,48,1024]{2,1,0:T(8,128)(2,1)} %bitcast.29), channel_id=1, source_target_pairs={{0,1},{1,0},{2,3},{3,2},{4,5},{5,4},{6,7},{7,6},{8,9},{9,8},{10,11... | collective-permute-start | bytes 294920 | tf_op jit(solution)/shard_map/ppermute | solution.py:18
  10.3 14.8 %all_gather.3 = bf16[192,1024]{1,0:T(8,128)(2,1)S(1)} all-gather(bf16[48,1024]{1,0:T(8,128)(2,1)} %param.5), channel_id=1, replica_groups=mesh['row'=8,'col'=4] {'col'}, dimensions={0}, use_global_device_ids=true | all-gather | bytes 491520 | tf_op jit(solution)/shard_map/all_gather | solution.py:53
  25.1 5.8 %convolution_convert_fusion.4 = bf16[192,3584]{1,0:T(8,128)(2,1)} fusion(bf16[192,1024]{1,0:T(8,128)(2,1)S(1)} %all_gather.3, bf16[1024,3584]{1,0:T(8,128)(2,1)} %param.8), kind=kOutput, calls=%fused_computation.6 | convolution fusion | flops 1409974272 | bytes 9109504 | tf_op jit(solution)/shard_map/dot_general | solution.py:62
  30.9 0.0 collective-permute-done
  31.0 0.8 collective-permute-start.1
  31.7 5.8 %convolution_convert_fusion.3 = bf16[192,3584]{1,0:T(8,128)(2,1)} fusion(bf16[192,1024]{1,0:T(8,128)(2,1)S(1)} %all_gather.3, bf16[1024,3584]{1,0:T(8,128)(2,1)} %param.7), kind=kOutput, calls=%fused_computation.5 | convolution fusion | flops 1409974272 | bytes 9109504 | tf_op jit(solution)/shard_map/dot_general | solution.py:58
  37.5 2.2 %collective-permute-done.1 = bf16[2,48,1024]{2,1,0:T(8,128)(2,1)S(1)} collective-permute-done((bf16[2,48,1024]{2,1,0:T(8,128)(2,1)S(1)}, bf16[2,48,1024]{2,1,0:T(8,128)(2,1)S(1)}, u32[]{:S(2)}, u32[]{:S(2)}) %collective-permute-start.1) | collective-permute-done | bytes 196640 | tf_op jit(solution)/shard_map/ppermute | solution.py:18
  39.8 0.1 reverse_select_fusion
  39.8 6.7 %convolution_convert_fusion.5 = bf16[192,3584]{1,0:T(8,128)(2,1)} fusion(bf16[192,1024]{1,0:T(8,128)(2,1)S(1)} %bitcast.26, bf16[3584,1024]{1,0:T(8,128)(2,1)} %param.9), kind=kOutput, calls=%fused_computation.7 | convolution fusion | flops 1409974272 | bytes 9109504 | tf_op jit(solution)/shard_map/dot_general | solution.py:36
  46.6 0.0 all-reduce.3.cloned.1.call-update
  46.6 0.2 reduce-scatter.2.cloned.1.call-start
  46.8 80.4 %all-reduce.3.cloned.1.call-done = (bf16[192,3584]{1,0:T(8,128)(2,1)}, bf16[192,3584]{1,0:T(8,128)(2,1)}, bf16[192,3584]{1,0:T(8,128)(2,1)}) async-done(((bf16[192,3584]{1,0:T(8,128)(2,1)}, bf16[192,3584]{1,0:T(8,128)(2,1)}, bf16[192,3584]{1,0:T(8,128)(2,1)}), (bf16[192,3584]{1,0:T(8,128)(2,1)}, bf16[192,3584]{1,0:T(8,128)(2,1)}, bf16[192,3584]{1,0:T(8,128)(2,1)})) %all-reduce.3.cloned.1.call-update) | async-done | bytes 4128784 | tf_op jit(solution)/shard_map/psum | solution.py:61
  127.2 7.1 %fusion.1 = bf16[1024,3584]{0,1:T(8,128)(2,1)} fusion(bf16[192,1024]{1,0:T(8,128)(2,1)S(1)} %all_gather.3, bf16[192,3584]{1,0:T(8,128)(2,1)} %get-tuple-element.10, bf16[192,3584]{1,0:T(8,128)(2,1)} %get-tuple-element.9), kind=kOutput, calls=%fused_computation.4 | convolution fusion | flops 1418461184 | bytes 10485760 | tf_op jit(solution)/shard_map/dot_general | solution.py:30
  134.2 0.0 slice-start
  134.3 1.2 fusion.4
  135.5 0.0 slice-start.1
  135.5 5.7 %fusion.20 = f32[192,1024]{1,0:T(8,128)S(1)} fusion(bf16[192,3584]{1,0:T(8,128)(2,1)S(1)} %fusion.4, bf16[1024,3584]{1,0:T(8,128)(2,1)} %param.7), kind=kOutput, calls=%fused_computation.34 | convolution fusion | flops 1409286144 | bytes 9502720 | tf_op jit(solution)/shard_map/dot_general | solution.py:36
  141.3 3.3 %fusion.14 = bf16[192,1024]{1,0:T(8,128)(2,1)} fusion(f32[192,1024]{1,0:T(8,128)S(1)} %fusion.20, bf16[1024,3584]{1,0:T(8,128)(2,1)S(1)} %bitcast.33, bf16[192,3584]{1,0:T(8,128)(2,1)S(1)} %copy-done.1, bf16[192,3584]{1,0:T(8,128)(2,1)S(1)} %copy-done.3), kind=kOutput, calls=%fused_computation.26 | convolution fusion | flops 1415184384 | bytes 11272192 | tf_op jit(solution)/shard_map/dot_general | solution.py:36
  144.6 0.0 reduce-scatter.2.cloned.1.call-update
  144.6 5.2 %fusion = bf16[1024,3584]{0,1:T(8,128)(2,1)} fusion(bf16[192,3584]{1,0:T(8,128)(2,1)S(1)} %fusion.4, bf16[192,1024]{1,0:T(8,128)(2,1)S(1)} %all_gather.3), kind=kOutput, calls=%fused_computation.3 | convolution fusion | flops 1412956160 | bytes 9109504 | tf_op jit(solution)/shard_map/dot_general | solution.py:30
  149.8 10.0 %copy.9 = bf16[1024,3584]{1,0:T(8,128)(2,1)} copy(bf16[1024,3584]{0,1:T(8,128)(2,1)} %fusion) | data formatting | bytes 14680064
  159.8 10.0 %copy.10 = bf16[1024,3584]{1,0:T(8,128)(2,1)} copy(bf16[1024,3584]{0,1:T(8,128)(2,1)} %fusion.1) | data formatting | bytes 14680064
  169.8 5.3 %convolution_convert_fusion = bf16[3584,1024]{1,0:T(8,128)(2,1)} fusion(bf16[192,1024]{1,0:T(8,128)(2,1)S(1)} %bitcast.27, bf16[192,3584]{1,0:T(8,128)(2,1)S(1)} %copy-done, bf16[192,3584]{1,0:T(8,128)(2,1)S(1)} %copy-done.2), kind=kOutput, calls=%fused_computation | convolution fusion | flops 1418461184 | bytes 10485760 | tf_op jit(solution)/shard_map/dot_general | solution.py:30
  (17 shorter events, 0.1 us)
Async XLA Ops:
  7.2 120.0 %all-reduce.3.cloned.1.call-start = ((), (), s32[]{:S(2)}) async-start(), calls=%async_computation.2 | async-start | bytes 8257536 | tf_op jit(solution)/shard_map/psum | solution.py:61
  7.2 23.7 %collective-permute-start = (bf16[1,48,1024]{2,1,0:T(8,128)(2,1)}, bf16[1,48,1024]{2,1,0:T(8,128)(2,1)S(1)}, u32[]{:S(2)}, u32[]{:S(2)}) collective-permute-start(bf16[1,48,1024]{2,1,0:T(8,128)(2,1)} %bitcast.29), channel_id=1, source_target_pairs={{0,1},{1,0},{2,3},{3,2},{4,5},{5,4},{6,7},{7,6},{8,9},{9,8},{10,11... | collective-permute-start | bytes 294920 | tf_op jit(solution)/shard_map/ppermute | solution.py:18
  25.1 5.8 %copy-start.4 = (bf16[48,1024]{1,0:T(8,128)(2,1)S(1)}, bf16[48,1024]{1,0:T(8,128)(2,1)}, u32[]{:S(2)}) copy-start(bf16[48,1024]{1,0:T(8,128)(2,1)} %param.6) | copy-start | bytes 294916
  31.0 8.7 %collective-permute-start.1 = (bf16[2,48,1024]{2,1,0:T(8,128)(2,1)S(1)}, bf16[2,48,1024]{2,1,0:T(8,128)(2,1)S(1)}, u32[]{:S(2)}, u32[]{:S(2)}) collective-permute-start(bf16[2,48,1024]{2,1,0:T(8,128)(2,1)S(1)} %get-tuple-element.12), channel_id=1, source_target_pairs={{0,2},{1,3},{2,0},{3,1},{4,6},{5,7},{6,4},{7,5},{8,10},{9,11},{10,... | collective-permute-start | bytes 589832 | tf_op jit(solution)/shard_map/ppermute | solution.py:18
  46.6 128.5 %reduce-scatter.2.cloned.1.call-start = ((), (), s32[]{:S(2)}) async-start(), calls=%async_computation.1 | async-start | bytes 491520 | tf_op jit(solution)/shard_map/reduce_scatter | solution.py:74
  127.2 7.1 %copy-start = (bf16[192,3584]{1,0:T(8,128)(2,1)S(1)}, bf16[192,3584]{1,0:T(8,128)(2,1)}, u32[]{:S(2)}) copy-start(bf16[192,3584]{1,0:T(8,128)(2,1)} %get-tuple-element.8) | copy-start | bytes 4128772
  127.2 7.1 %copy-start.1 = (bf16[192,3584]{1,0:T(8,128)(2,1)S(1)}, bf16[192,3584]{1,0:T(8,128)(2,1)}, u32[]{:S(2)}) copy-start(bf16[192,3584]{1,0:T(8,128)(2,1)} %get-tuple-element.10) | copy-start | bytes 4128772
  127.2 7.1 %copy-start.3 = (bf16[192,3584]{1,0:T(8,128)(2,1)S(1)}, bf16[192,3584]{1,0:T(8,128)(2,1)}, u32[]{:S(2)}) copy-start(bf16[192,3584]{1,0:T(8,128)(2,1)} %get-tuple-element.9) | copy-start | bytes 4128772
  134.2 7.0 %slice-start = ((s8[7340032]{0:T(1024)(128)(4,1)}), s8[4194304]{0:T(1024)(128)(4,1)S(1)}, s32[]{:S(2)}) async-start(s8[7340032]{0:T(1024)(128)(4,1)} %bitcast.32), calls=%async_computation.3 | async-start | bytes 8388608
  135.5 5.8 %slice-start.1 = ((s8[7340032]{0:T(1024)(128)(4,1)}), s8[3145728]{0:T(1024)(128)(4,1)S(1)}, s32[]{:S(2)}) async-start(s8[7340032]{0:T(1024)(128)(4,1)} %bitcast.32), calls=%async_computation.4 | async-start | bytes 6291456
  159.8 10.0 %copy-start.2 = (bf16[192,3584]{1,0:T(8,128)(2,1)S(1)}, bf16[192,3584]{1,0:T(8,128)(2,1)}, u32[]{:S(2)}) copy-start(bf16[192,3584]{1,0:T(8,128)(2,1)} %get-tuple-element.10) | copy-start | bytes 4128772
Sparse Core Ops, SparseCore 0:
  46.7 80.4 all-reduce.2
  144.8 20.8 reduce-scatter.1
